TPU v7x, 512 devices: a whole 4x4x16 slice. The times are simulated.
512 devices in a mesh: fit: 32 (over z, core), orb: 16 (over x, y).
Axes of the slice: x: 4, y: 4, z: 16, core: 2. Of those that a mesh axis runs over, the one named last changes fastest.
Arguments:
- half_ints: bfloat16 [16, 256, 768, 256], P('orb', None, 'fit'), may hold values from -6 to 6
- osv_coef: bfloat16 [16, 256, 256, 64], P('orb', 'fit'), may hold values from -0.09375 to 0.09375
- fit_blocks: int32 [16, 256, 6], P('orb', 'fit'), may hold values from 0 to 468, as said below
- partner_list: int32 [32, 16, 24], P('fit'), may hold values from 0 to 127, as said below
Outputs:
- pair_ints: bfloat16 [16, 256, 24, 4096], P('orb', 'fit')
Inputs may be any that keep to these rules, and one draw needn't show every extreme that they name: `fit_blocks`: the 6 block numbers of one orbital are distinct. `partner_list`: entry h * 8 + k names orbital k of the same column in group h. The 24 entries of one list are distinct. Of one list, at most 3 entries name orbitals of any one group, and in every list some group is named exactly 3 times.
All inputs are finite; a program needn't handle non-finite values.
Results may differ from a plain program's by a relative error of at most 0.0055.
Values may be sent and summed in bfloat16 or wider, within the bound.
No kernel may reach another device: no remote copies, remote signals or barrier semaphores. Data moves between devices by JAX's collectives and lax.ppermute only.
A program may use at most 64 MiB of HBM per device.

v0:
```python
import jax
import jax.numpy as jnp
from jax import lax
from jax.sharding import PartitionSpec as P

BLK = 128
FBLK = 6


def per_device(half_ints, osv_coef, fit_blocks, partner_list):
    local_rows = half_ints[0]
    own_ints = lax.all_to_all(local_rows, "fit", split_axis=0, concat_axis=1, tiled=True)
    osv_local = osv_coef[0]
    projected = jnp.einsum(
        "kfa,kao->kof", own_ints, osv_local, preferred_element_type=jnp.float32
    ).astype(jnp.bfloat16)
    own_blocks = fit_blocks[0]
    column_lists = partner_list[0]
    nosv_count = projected.shape[1]
    npart_count = column_lists.shape[1]
    my_group = lax.axis_index("orb")
    wanted = lax.dynamic_index_in_dim(column_lists, my_group, 0, keepdims=False)
    piece_rows = lax.all_gather(projected, "orb", axis=0, tiled=True)
    piece_blocks = lax.all_gather(own_blocks, "orb", axis=0, tiled=True)
    piece_len = piece_rows.shape[0]
    matches = wanted[:, None] == jnp.arange(piece_len, dtype=jnp.int32)[None, :]
    buffer = jnp.einsum(
        "nr,rxf->nxf", matches.astype(jnp.bfloat16), piece_rows, preferred_element_type=jnp.float32
    ).astype(jnp.bfloat16)
    blocks = jnp.sum(jnp.where(matches[:, :, None], piece_blocks[None, :, :], 0), axis=1).astype(
        jnp.int32
    )
    partner_pieces = buffer.reshape(npart_count, nosv_count, FBLK, BLK)

    def pair_block(operand):
        own_rows, own_ids = operand
        matching = (own_ids[None, :, None] == blocks[:, None, :]).astype(jnp.bfloat16)
        aligned = jnp.einsum(
            "nbc,nxcp->nxbp", matching, partner_pieces, preferred_element_type=jnp.float32
        ).astype(jnp.bfloat16)
        pair_vals = jnp.einsum(
            "abp,nxbp->nax",
            own_rows.reshape(nosv_count, FBLK, BLK),
            aligned,
            preferred_element_type=jnp.float32,
        )
        return pair_vals.astype(jnp.bfloat16).reshape(npart_count, nosv_count * nosv_count)

    result = lax.map(pair_block, (projected, own_blocks))
    return result[None]


def solution(mesh):
    return jax.shard_map(
        per_device,
        mesh=mesh,
        in_specs=(
            P("orb", None, "fit", None),
            P("orb", "fit", None, None),
            P("orb", "fit", None),
            P("fit", None, None),
        ),
        out_specs=P("orb", "fit", None, None),
        check_vma=False,
    )
```

profile of v0, /device:TPU:1, one launch (start us, length us, event | category | flops | bytes accessed | tf_op | source)
XLA Modules:
  0.0 406.4 jit_solution(8026830469797910473)
XLA Ops:
  6.5 162.5 %all_to_all.18 = bf16[256,24,256]{2,1,0:T(8,128)(2,1)S(1)} all-to-all(bf16[256,24,256]{2,1,0:T(8,128)(2,1)} %bitcast.55), channel_id=1, replica_groups=mesh['fit'=32,'orb'=16] {'fit'}, dimensions={0} | all-to-all | bytes 6291456 | tf_op jit(solution)/shard_map/all_to_all | solution.py:12
  169.2 2.0 convolution_convert_fusion
  171.4 19.8 %all-gather = s32[1,128,6]{2,0,1:T(1,128)S(1)} all-gather(s32[1,8,6]{2,0,1:T(1,128)S(1)} %copy.31), channel_id=2, replica_groups=mesh['fit'=32,'orb'=16] {'orb'}, dimensions={1}, use_global_device_ids=true | all-gather | bytes 3264 | tf_op jit(solution)/shard_map/all_gather | solution.py:24
  192.4 75.6 %all-gather.3.cloned.1.call-done = bf16[128,64,768]{2,1,0:T(8,128)(2,1)} async-done(((bf16[8,64,768]{2,1,0:T(8,128)(2,1)}), bf16[128,64,768]{2,1,0:T(8,128)(2,1)}) %all-gather.3.cloned.1.call-update) | async-done | bytes 12582928 | tf_op jit(solution)/shard_map/all_gather | solution.py:23
  268.0 18.0 %fusion.20 = bf16[24,64,768]{2,0,1:T(8,128)(2,1)S(1)} fusion(bf16[128,64,768]{2,1,0:T(8,128)(2,1)} %all-gather.3.cloned.1.call-done, s32[24]{0:T(128)S(1)} %dynamic-slice_bitcast_fusion), kind=kOutput, calls=%fused_computation.18 | convolution fusion | flops 303172608 | bytes 14942304 | tf_op jit(solution)/shard_map/nr,rxf->nxf/dot_general | solution.py:27
  286.0 1.9 copy.35
  287.9 4.8 %reshape.40 = bf16[24,64,6,128]{3,2,1,0:T(8,128)(2,1)S(1)} reshape(bf16[24,64,768]{2,1,0:T(8,128)(2,1)} %copy.35) | data formatting | bytes 4718592 | tf_op jit(solution)/shard_map/reshape | solution.py:33
  292.8 106.8 %while.10 = (s32[]{:T(128)}, bf16[8,24,4096]{2,1,0:T(8,128)(2,1)}, s32[8,6]{1,0:T(8,128)S(1)}, s32[24,6]{1,0:T(8,128)S(1)}, bf16[24,64,6,128]{3,2,1,0:T(8,128)(2,1)S(1)}, /*index=5*/bf16[8,64,768]{2,1,0:T(8,128)(2,1)}, s32[]{:T(128)}) while((s32[]{:T(128)}, bf16[8,24,4096]{2,1,0:T(8,128)(2,1)}, s32[8,6]{1,0:T(8,128)S(1)}, ...), condition=%wide.region_2.3_spmd, body=%wide.region_1.2_spmd.sunk | while | flops 166429536 | bytes 8946909 | solution.py:49
  292.8 2.7 convert_bitcast_fusion.2
  297.1 3.4 fusion.38
  302.5 2.0 broadcast_in_dim.45
  306.1 2.7 convert_bitcast_fusion.2
  310.5 3.4 fusion.38
  315.8 2.0 broadcast_in_dim.45
  319.5 2.7 convert_bitcast_fusion.2
  323.8 3.4 fusion.38
  329.2 2.0 broadcast_in_dim.45
  332.8 2.7 convert_bitcast_fusion.2
  337.2 3.4 fusion.38
  342.5 2.0 broadcast_in_dim.45
  346.2 2.7 convert_bitcast_fusion.2
  350.5 3.4 fusion.38
  355.9 2.0 broadcast_in_dim.45
  359.5 2.7 convert_bitcast_fusion.2
  363.9 3.4 fusion.38
  369.2 2.0 broadcast_in_dim.45
  372.9 2.7 convert_bitcast_fusion.2
  377.2 3.4 fusion.38
  382.6 2.0 broadcast_in_dim.45
  386.2 2.7 convert_bitcast_fusion.2
  390.6 3.4 fusion.38
  395.9 2.0 broadcast_in_dim.45
  (55 shorter events, 43.3 us)
Async XLA Ops:
  6.5 162.7 %copy-start = (bf16[1,8,256,64]{2,3,1,0:T(8,128)(2,1)S(1)}, bf16[1,8,256,64]{2,3,1,0:T(8,128)(2,1)}, u32[]{:S(2)}) copy-start(bf16[1,8,256,64]{2,3,1,0:T(8,128)(2,1)} %param.7) | copy-start | bytes 786436
  6.5 261.4 %all-gather.3.cloned.1.call-start = ((), (), s32[]{:S(2)}) async-start(), calls=%async_computation.1 | async-start | bytes 13369344 | tf_op jit(solution)/shard_map/all_gather | solution.py:23
  169.2 2.1 copy-start.1
Sparse Core Ops, SparseCore 0:
  171.4 96.5 all-gather.2
where the time goes:
time: 408 us; the launch traced here: 406 us
  blocking collectives  182 us (45%)
  waiting for transfers between devices  75.6 us (19%)
  matrix products  68.8 us (17%)
  local copies, waits for them, and re-layouts  66 us (16%)
  between operations  13.5 us (3%)
    all_to_all x1, blocking collectives, per_device(): lax.all_to_all(local_rows, 'fit', split_axis=0, concat_axis=1, tiled=True)  162 us
    all_gather x1, waiting for transfers between devices, per_device(): piece_rows = lax.all_gather(projected, 'orb', axis=0, tiled=True)  75.6 us
    dot_general x8, matrix products, pair_block(): jnp.einsum('abp,nxbp->nax', own_rows.reshape(nosv_count, FBLK, BLK), alig...  27.3 us
    dot_general x8, matrix products, pair_block(): jnp.einsum('nbc,nxcp->nxbp', matching, partner_pieces, preferred_element_...  21.5 us
    all_gather x1, blocking collectives, per_device(): piece_blocks = lax.all_gather(own_blocks, 'orb', axis=0, tiled=True)  19.8 us
    dot_general x1, matrix products, per_device(): jnp.einsum('nr,rxf->nxf', matches.astype(jnp.bfloat16), piece_rows, prefe...  18 us
    broadcast_in_dim x8, local copies, waits for them, and re-layouts, per_device(): result = lax.map(pair_block, (projected, own_blocks))  16.3 us
    convert_element_type x8, local copies, waits for them, and re-layouts, pair_block(): pair_vals.astype(jnp.bfloat16).reshape(npart_count, nosv_count * nosv_count)  15.4 us
  transfers between devices with their start and end apart: 1, of which 1 were waited for; matrix products, arithmetic and copies ran while one was open for 0% of the time, Pallas kernels for 0%

commit v1 on v0

--- a/solution.py
+++ b/solution.py
@@ -9,7 +9,10 @@
 
 def per_device(half_ints, osv_coef, fit_blocks, partner_list):
     local_rows = half_ints[0]
-    own_ints = lax.all_to_all(local_rows, "fit", split_axis=0, concat_axis=1, tiled=True)
+    own_ints = jnp.concatenate(
+        lax.all_to_all(jnp.stack(jnp.split(local_rows, lax.axis_size("fit"), axis=0)), "fit", 0, 0),
+        axis=1,
+    )
     osv_local = osv_coef[0]
     projected = jnp.einsum(
         "kfa,kao->kof", own_ints, osv_local, preferred_element_type=jnp.float32

time: 408 us -> 437 us (1.071)
  local copies, waits for them, and re-layouts: 66 us -> 94.8 us
    unnamed x6 -> x37, local copies, waits for them, and re-layouts: 0.17 us -> 28.1 us
where the time goes in v1:
time: 437 us; the launch traced here: 435 us
  blocking collectives  182 us (42%)
  local copies, waits for them, and re-layouts  94.8 us (22%)
  waiting for transfers between devices  75.6 us (17%)
  matrix products  68.8 us (16%)
  between operations  13.5 us (3%)
    all_to_all x1, blocking collectives, per_device(): lax.all_to_all(jnp.stack(jnp.split(local_rows, lax.axis_size('fit'), axis...  162 us
    all_gather x1, waiting for transfers between devices, per_device(): piece_rows = lax.all_gather(projected, 'orb', axis=0, tiled=True)  75.6 us
    unnamed x37, local copies, waits for them, and re-layouts  28.1 us
    dot_general x8, matrix products, pair_block(): jnp.einsum('abp,nxbp->nax', own_rows.reshape(nosv_count, FBLK, BLK), alig...  27.3 us
    dot_general x8, matrix products, pair_block(): jnp.einsum('nbc,nxcp->nxbp', matching, partner_pieces, preferred_element_...  21.5 us
    all_gather x1, blocking collectives, per_device(): piece_blocks = lax.all_gather(own_blocks, 'orb', axis=0, tiled=True)  19.8 us
    dot_general x1, matrix products, per_device(): jnp.einsum('nr,rxf->nxf', matches.astype(jnp.bfloat16), piece_rows, prefe...  18 us
    broadcast_in_dim x8, local copies, waits for them, and re-layouts, per_device(): result = lax.map(pair_block, (projected, own_blocks))  16.3 us
  transfers between devices with their start and end apart: 1, of which 1 were waited for; matrix products, arithmetic and copies ran while one was open for 0% of the time, Pallas kernels for 0%

profile of v1, /device:TPU:1, one launch (start us, length us, event | category | flops | bytes accessed | tf_op | source)
XLA Modules:
  0.0 434.9 jit_solution(3600475967406332993)
XLA Ops:
  35.4 162.1 %all_to_all.5 = bf16[32,8,24,256]{3,2,1,0:T(8,128)(2,1)S(1)} all-to-all(bf16[32,8,24,256]{3,2,1,0:T(8,128)(2,1)S(1)} %slice_dynamic-update-slice_fusion), channel_id=1, replica_groups=mesh['fit'=32,'orb'=16] {'fit'}, dimensions={0} | all-to-all | bytes 6291456 | tf_op jit(solution)/shard_map/all_to_all | solution.py:13
  197.7 2.0 fusion.23
  199.9 19.8 %all-gather = s32[1,128,6]{2,0,1:T(1,128)S(1)} all-gather(s32[1,8,6]{2,0,1:T(1,128)S(1)} %copy.31), channel_id=2, replica_groups=mesh['fit'=32,'orb'=16] {'orb'}, dimensions={1}, use_global_device_ids=true | all-gather | bytes 3264 | tf_op jit(solution)/shard_map/all_gather | solution.py:27
  220.9 75.6 %all-gather.3.cloned.1.call-done = bf16[128,64,768]{2,1,0:T(8,128)(2,1)} async-done(((bf16[8,64,768]{2,1,0:T(8,128)(2,1)}), bf16[128,64,768]{2,1,0:T(8,128)(2,1)}) %all-gather.3.cloned.1.call-update) | async-done | bytes 12582928 | tf_op jit(solution)/shard_map/all_gather | solution.py:26
  296.5 18.0 %fusion.20 = bf16[24,64,768]{2,0,1:T(8,128)(2,1)S(1)} fusion(bf16[128,64,768]{2,1,0:T(8,128)(2,1)} %all-gather.3.cloned.1.call-done, s32[24]{0:T(128)S(1)} %dynamic-slice_bitcast_fusion), kind=kOutput, calls=%fused_computation.18 | convolution fusion | flops 303172608 | bytes 14942304 | tf_op jit(solution)/shard_map/nr,rxf->nxf/dot_general | solution.py:30
  314.5 1.9 copy.35
  316.4 4.8 %reshape.112 = bf16[24,64,6,128]{3,2,1,0:T(8,128)(2,1)S(1)} reshape(bf16[24,64,768]{2,1,0:T(8,128)(2,1)} %copy.35) | data formatting | bytes 4718592 | tf_op jit(solution)/shard_map/reshape | solution.py:36
  321.2 106.8 %while.10 = (s32[]{:T(128)}, bf16[8,24,4096]{2,1,0:T(8,128)(2,1)}, s32[8,6]{1,0:T(8,128)S(1)}, s32[24,6]{1,0:T(8,128)S(1)}, bf16[24,64,6,128]{3,2,1,0:T(8,128)(2,1)S(1)}, /*index=5*/bf16[8,64,768]{2,1,0:T(8,128)(2,1)}, s32[]{:T(128)}) while((s32[]{:T(128)}, bf16[8,24,4096]{2,1,0:T(8,128)(2,1)}, s32[8,6]{1,0:T(8,128)S(1)}, ...), condition=%wide.region_2.3_spmd, body=%wide.region_1.2_spmd.sunk | while | flops 166429536 | bytes 8946909 | solution.py:52
  321.3 2.7 convert_bitcast_fusion.2
  325.6 3.4 fusion.39
  331.0 2.0 broadcast_in_dim.45
  334.6 2.7 convert_bitcast_fusion.2
  339.0 3.4 fusion.39
  344.3 2.0 broadcast_in_dim.45
  348.0 2.7 convert_bitcast_fusion.2
  352.3 3.4 fusion.39
  357.7 2.0 broadcast_in_dim.45
  361.3 2.7 convert_bitcast_fusion.2
  365.7 3.4 fusion.39
  371.0 2.0 broadcast_in_dim.45
  374.7 2.7 convert_bitcast_fusion.2
  379.0 3.4 fusion.39
  384.4 2.0 broadcast_in_dim.45
  388.0 2.7 convert_bitcast_fusion.2
  392.4 3.4 fusion.39
  397.7 2.0 broadcast_in_dim.45
  401.4 2.7 convert_bitcast_fusion.2
  405.7 3.4 fusion.39
  411.1 2.0 broadcast_in_dim.45
  414.7 2.7 convert_bitcast_fusion.2
  419.1 3.4 fusion.39
  424.4 2.0 broadcast_in_dim.45
  (87 shorter events, 72.1 us)
Async XLA Ops:
  6.5 191.2 %copy-start = (bf16[1,8,256,64]{2,3,1,0:T(8,128)(2,1)S(1)}, bf16[1,8,256,64]{2,3,1,0:T(8,128)(2,1)}, u32[]{:S(2)}) copy-start(bf16[1,8,256,64]{2,3,1,0:T(8,128)(2,1)} %param.7) | copy-start | bytes 786436
  6.5 289.9 %all-gather.3.cloned.1.call-start = ((), (), s32[]{:S(2)}) async-start(), calls=%async_computation.1 | async-start | bytes 13369344 | tf_op jit(solution)/shard_map/all_gather | solution.py:26
  197.7 2.1 copy-start.1
Sparse Core Ops, SparseCore 0:
  199.9 96.5 all-gather.2
